TPU v7x, 256 devices: a whole 4x4x8 slice. The times are simulated.
256 devices in a mesh: row: 8 (over y, core), col: 32 (over z, x).
Axes of the slice: x: 4, y: 4, z: 8, core: 2. Of those that a mesh axis runs over, the one named last changes fastest.
Arguments:
- blocks: float32 [128, 32, 256, 256], P('row', 'col'), may hold values from -6 to 6
- panel_rows: int32 [2, 64], P(None, 'row'), may hold values from -1 to 767, as said below
- target_slots: int32 [2, 128, 32], P(None, 'row', 'col'), may hold values from -1 to 7, as said below
- diag_inverse: float32 [2, 256, 256], replicated, may hold values from -1 to 1, as said below
- cross_block: float32 [256, 256], replicated, may hold values from -6 to 6
Outputs:
- factored: float32 [128, 32, 256, 256], P('row', 'col')
Inputs may be any that keep to these rules, and one draw needn't show every extreme that they name: `panel_rows`: slot q * 2 + m of row device r stands for the m-th structure row of block column class r + q times the number of row devices; both lists are -1 where that class is 0 or 1, and list 0 is -1 also where block column 0 lacks the row; otherwise list 0 equals list 1. `target_slots`: A filled slot of class c names in entry 0 a slot of its own row device and in entry 1 a slot of row device c modulo the number of row devices, within (c // number of row devices) * 2 and the 1 after it; both are filled or both -1, always -1 in classes 0 and 1; the target's block row number is at least its block column number. `diag_inverse`: each matrix is lower triangular.
All inputs are finite; a program needn't handle non-finite values.
Results may differ from a plain program's by a relative error of at most 0.0003.
Values sent between devices are 32-bit elements; how exact they have to be, the bound alone decides.
No kernel may reach another device: no remote copies, remote signals or barrier semaphores. Data moves between devices by JAX's collectives and lax.ppermute only.
A program may use at most 128 MiB of HBM per device.

v0:
```python
import jax
import jax.numpy as jnp
from jax import lax
from jax.sharding import PartitionSpec as P

PER_CLASS = 2
HIGHEST_PRECISION = lax.Precision.HIGHEST


def broadcast(array, axis, root):
    mine = lax.axis_index(axis) == root
    return lax.psum(jnp.where(mine, array, jnp.zeros_like(array)), axis)


def apply_inverse(panel_blocks, inverse):
    return jnp.einsum("sab,cb->sac", panel_blocks, inverse, precision=HIGHEST_PRECISION)


def per_device(blocks, panel_rows, target_slots, diag_inverse, cross_block):
    column = lax.axis_index("col")
    row_count = lax.axis_size("row")
    stored = blocks[:, 0]
    slot_count = panel_rows.shape[1]
    head_part = stored[:slot_count]
    first_live = (panel_rows[0] >= 0)[:, None, None]
    second_live = (panel_rows[1] >= 0)[:, None, None]
    cross_factor = jnp.dot(cross_block, diag_inverse[0].T, precision=HIGHEST_PRECISION)
    blank_part = jnp.zeros_like(head_part)
    class_start = column // row_count * PER_CLASS
    owner_row = column % row_count
    first_factor = lax.cond(
        column == 0,
        lambda: jnp.where(first_live, apply_inverse(head_part, diag_inverse[0]), 0.0),
        lambda: blank_part,
    )
    first_rows = broadcast(first_factor, "col", 0)
    first_cols = broadcast(
        lax.dynamic_slice_in_dim(first_rows, class_start, PER_CLASS, 0), "row", owner_row
    )
    second_factor = lax.cond(
        column == 1,
        lambda: jnp.where(
            second_live,
            apply_inverse(head_part - apply_inverse(first_rows, cross_factor), diag_inverse[1]),
            0.0,
        ),
        lambda: blank_part,
    )
    second_rows = broadcast(second_factor, "col", 1)
    second_cols = broadcast(
        lax.dynamic_slice_in_dim(second_rows, class_start, PER_CLASS, 0), "row", owner_row
    )
    row_index = target_slots[0, :, 0]
    col_index = target_slots[1, :, 0]
    present = row_index >= 0
    left_slot = jnp.where(present, row_index, 0)
    right_slot = jnp.where(present, col_index - class_start, 0)
    left_blocks = jnp.concatenate([first_rows[left_slot], second_rows[left_slot]], axis=2)
    right_blocks = jnp.concatenate([first_cols[right_slot], second_cols[right_slot]], axis=2)
    schur_term = jnp.einsum("sak,sbk->sab", left_blocks, right_blocks, precision=HIGHEST_PRECISION)
    trailing = stored - jnp.where(present[:, None, None], schur_term, 0.0)
    own_panel = jnp.where(column == 0, first_factor, second_factor)
    keep_mask = (column == 0) & first_live | (column == 1) & second_live
    head_blocks = jnp.where(keep_mask, own_panel, trailing[:slot_count])
    factored = jnp.concatenate([head_blocks, trailing[slot_count:]], axis=0)
    return factored[:, None]


def solution(mesh):
    return jax.shard_map(
        per_device,
        mesh=mesh,
        in_specs=(P("row", "col", None, None), P(None, "row"), P(None, "row", "col"), P(), P()),
        out_specs=P("row", "col", None, None),
        check_vma=False,
    )
```

profile of v0, /device:TPU:2, one launch (start us, length us, event | category | flops | bytes accessed | tf_op | source)
XLA Modules:
  0.0 431.3 jit_solution(9175127619029981087)
XLA Ops:
  6.5 3.1 slice_bitcast_fusion
  9.7 0.2 conditional.2
  9.9 1.8 broadcast_select_fusion.1
  11.7 0.3 copy-done.3
  12.1 0.4 fusion.22
  12.5 155.4 %all-reduce.5.cloned.1.call-done = f32[8,256,256]{2,1,0:T(8,128)} async-done(((f32[8,256,256]{2,1,0:T(8,128)}), f32[8,256,256]{2,1,0:T(8,128)}) %all-reduce.5.cloned.1.call-update) | async-done | bytes 2097168 | tf_op jit(solution)/shard_map/psum | solution.py:12
  167.9 5.5 %conditional.3 = (f32[8,256,256]{2,1,0:T(8,128)S(1)}) conditional(s32[]{:T(128)} %convert_element_type.7, () %tuple.19, (s32[1,8]{1,0:T(1,128)S(1)}, s32[]{:T(128)}, f32[8,256,256]{2,1,0:T(8,128)}, f32[256,256]{1,0:T(8,128)S(1)}, f32[8,256,256]{2,1,0:T(8,128)}, /*index=5*/f32[2,256,256]{2,1,0:T(8,128)S(1)}) %tuple.37), branch_computations={%region_3.4_spmd, %region_4.5_spmd} | conditional | flops 3222274048 | bytes 19399248 | solution.py:40
  167.9 3.7 fusion.8
  171.6 1.8 fusion.4
  173.4 1.3 copy-done.5
  174.7 1.5 broadcast_select_fusion
  176.3 0.2 all-reduce.9.cloned.1.call-start
  176.6 1.3 copy-done.2
  177.9 0.8 dynamic-slice_select_fusion.1
  178.7 145.2 %all-reduce.7.cloned.1.call-done = f32[8,256,256]{2,1,0:T(8,128)} async-done(((f32[8,256,256]{2,1,0:T(8,128)}), f32[8,256,256]{2,1,0:T(8,128)}) %all-reduce.7.cloned.1.call-update) | async-done | bytes 2097168 | tf_op jit(solution)/shard_map/psum | solution.py:12
  323.8 1.9 dynamic-slice_select_fusion
  325.8 2.8 gather_fusion
  328.6 4.3 %gather_fusion.1 = f32[16,256,256]{2,1,0:T(8,128)} fusion(f32[8,256,256]{2,1,0:T(8,128)} %all-reduce.7.cloned.1.call-done, s32[1024]{0:T(1024)S(1)} %get-tuple-element.51), kind=kCustom, calls=%fused_computation.1 | custom fusion | bytes 8388672 | tf_op jit(solution)/shard_map/gather | solution.py:58
  332.9 59.6 %all-reduce.9.cloned.1.call-done = (f32[2,256,256]{2,1,0:T(8,128)}, f32[2,256,256]{2,1,0:T(8,128)}) async-done(((f32[2,256,256]{2,1,0:T(8,128)}, f32[2,256,256]{2,1,0:T(8,128)}), (f32[2,256,256]{2,1,0:T(8,128)}, f32[2,256,256]{2,1,0:T(8,128)})) %all-reduce.9.cloned.1.call-update) | async-done | bytes 1048592 | tf_op jit(solution)/shard_map/psum | solution.py:12
  392.6 3.9 gather_fusion.3
  396.5 2.8 gather_fusion.2
  399.3 22.5 %bitcast_subtract_fusion = f32[16,256,256]{2,1,0:T(8,128)S(1)} fusion(f32[16,1,256,256]{3,2,1,0:T(8,128)} %param.9, pred[16]{0:T(512)(128)(4,1)S(1)} %compare_bitcast_fusion.1, f32[16,256,256]{2,1,0:T(8,128)} %gather_fusion.3, f32[16,256,256]{2,1,0:T(8,128)} %gather_fusion.2, f32[16,256,256]{2,1,0:T(8,128)} %gather_fusion.1, f32[16,256,256]{2,1,0:T(8,128)} %gather_fusion), kind=kOutput, calls=%fused_computation.23 | convolution fusion | flops 6448742400 | bytes 25165840 | tf_op jit(solution)/shard_map/sak,sbk->sab/dot_general | solution.py:60
  421.7 0.6 slice_select_fusion
  422.3 2.4 maximum_bitcast_fusion
  (31 shorter events, 0.3 us)
Async XLA Ops:
  6.5 5.5 %copy-start = (f32[256,256]{1,0:T(8,128)S(1)}, f32[256,256]{1,0:T(8,128)}, u32[]{:S(2)}) copy-start(f32[256,256]{1,0:T(8,128)} %param.13) | copy-start | bytes 786436
  6.5 161.3 %all-reduce.5.cloned.1.call-start = ((), (), s32[]{:S(2)}) async-start(), calls=%async_computation | async-start | bytes 4194304 | tf_op jit(solution)/shard_map/psum | solution.py:12
  6.5 3.1 copy-start.9
  6.5 3.1 copy-start.8
  9.9 2.1 copy-start.3
  12.0 311.8 %all-reduce.7.cloned.1.call-start = ((), (), s32[]{:S(2)}) async-start(), calls=%async_computation.1 | async-start | bytes 4194304 | tf_op jit(solution)/shard_map/psum | solution.py:12
  167.9 3.7 copy-start.7
  173.4 1.3 copy-start.5
  176.3 1.6 copy-start.2
  176.3 149.4 %copy-start.10 = (s32[2,16,1]{1,2,0:T(1,128)S(1)}, s32[2,16,1]{1,2,0:T(1,128)}, u32[]{:S(2)}) copy-start(s32[2,16,1]{1,2,0:T(1,128)} %param.11) | copy-start | bytes 388
  176.3 216.2 %all-reduce.9.cloned.1.call-start = ((), (), s32[]{:S(2)}) async-start(), calls=%async_computation.2 | async-start | bytes 2097152 | tf_op jit(solution)/shard_map/psum | solution.py:12
  392.5 3.9 copy-start.1
  399.3 22.5 %copy-start.4 = (f32[8,256,256]{2,1,0:T(8,128)S(1)}, f32[8,256,256]{2,1,0:T(8,128)}, u32[]{:S(2)}) copy-start(f32[8,256,256]{2,1,0:T(8,128)} %copy-done.3) | copy-start | bytes 6291460
  399.3 22.5 %copy-start.6 = (f32[8,256,256]{2,1,0:T(8,128)S(1)}, f32[8,256,256]{2,1,0:T(8,128)}, u32[]{:S(2)}) copy-start(f32[8,256,256]{2,1,0:T(8,128)} %copy-done.5) | copy-start | bytes 6291460
Sparse Core Ops, SparseCore 0:
  12.1 155.7 all-reduce.4
  176.4 147.3 all-reduce.6
  326.3 66.2 all-reduce.8
where the time goes:
time: 432 us; the launch traced here: 431 us
  waiting for transfers between devices  360 us (83%)
  matrix products  28.4 us (7%)
  local copies, waits for them, and re-layouts  20 us (5%)
  between operations  13.3 us (3%)
  other arithmetic  9.08 us (2%)
    psum x3, waiting for transfers between devices, broadcast(): return lax.psum(jnp.where(mine, array, jnp.zeros_like(array)), axis)  360 us
    dot_general x1, matrix products, per_device(): jnp.einsum('sak,sbk->sab', left_blocks, right_blocks, precision=HIGHEST_P...  22.5 us
  transfers between devices with their start and end apart: 3, of which 3 were waited for; matrix products, arithmetic and copies ran while one was open for 2% of the time, Pallas kernels for 0%

commit v1 on v0

--- a/solution.py
+++ b/solution.py
@@ -9,7 +9,7 @@
 
 def broadcast(array, axis, root):
     mine = lax.axis_index(axis) == root
-    return lax.psum(jnp.where(mine, array, jnp.zeros_like(array)), axis)
+    return jnp.sum(lax.all_gather(jnp.where(mine, array, jnp.zeros_like(array)), axis), axis=0)
 
 
 def apply_inverse(panel_blocks, inverse):

time: 432 us -> 1010 us (2.34)
  waiting for transfers between devices: 360 us -> 890 us
  other arithmetic: 9.08 us -> 59.5 us
    all_gather x0 -> x4, waiting for transfers between devices: none -> 890 us  [broadcast(): lax.all_gather(jnp.where(mine, array, jnp.zeros_like(array)), axis)]
    psum x3 -> x0, waiting for transfers between devices: 360 us -> none  [broadcast(): return lax.psum(jnp.where(mine, array, jnp.zeros_like(array)), axis)]
    reduce_sum x0 -> x4, other arithmetic: none -> 48.9 us  [broadcast(): jnp.sum(lax.all_gather(jnp.where(mine, array, jnp.zeros_like(array)), axi...]
  transfers between devices with their start and end apart: 3 -> 4, of which waited for: 3 -> 4; matrix products, arithmetic and copies ran while one was open for 2% -> 4% of each run, Pallas kernels for 0% -> 0%
where the time goes in v1:
time: 1010 us
  waiting for transfers between devices  890 us (88%)
  other arithmetic  59.5 us (6%)
  matrix products  28 us (3%)
  local copies, waits for them, and re-layouts  16.3 us (2%)
  between operations  13.3 us (1%)
    all_gather x4, waiting for transfers between devices, broadcast(): lax.all_gather(jnp.where(mine, array, jnp.zeros_like(array)), axis)  890 us
    reduce_sum x4, other arithmetic, broadcast(): jnp.sum(lax.all_gather(jnp.where(mine, array, jnp.zeros_like(array)), axi...  48.9 us
    dot_general x1, matrix products, per_device(): jnp.einsum('sak,sbk->sab', left_blocks, right_blocks, precision=HIGHEST_P...  22.5 us
  transfers between devices with their start and end apart: 4, of which 4 were waited for; matrix products, arithmetic and copies ran while one was open for 4% of the time, Pallas kernels for 0%

profile of v1, /device:TPU:2, one launch (start us, length us, event | category | flops | bytes accessed | tf_op | source)
XLA Modules:
  0.0 1007.8 jit_solution(6423230128452729083)
XLA Ops:
  6.5 3.1 slice_bitcast_fusion
  9.9 1.7 broadcast_select_fusion.1
  11.9 0.4 fusion.22
  12.3 432.7 %all-gather.9.cloned.1.call-done = f32[256,256,256]{2,1,0:T(8,128)} async-done(((f32[8,256,256]{2,1,0:T(8,128)}), f32[256,256,256]{2,1,0:T(8,128)}) %all-gather.9.cloned.1.call-update) | async-done | bytes 67108880 | tf_op jit(solution)/shard_map/all_gather | solution.py:12
  445.1 20.8 %reduce_sum.36 = f32[8,256,256]{2,1,0:T(8,128)S(1)} reduce(f32[32,8,256,256]{3,2,1,0:T(8,128)} %bitcast.10, f32[]{:T(128)} %constant.47.clone.1), dimensions={0}, to_apply=%region_2.3 | reduce | flops 16252928 | bytes 69206016 | tf_op jit(solution)/shard_map/reduce_sum | solution.py:12
  465.9 5.2 conditional.3
  465.9 1.9 fusion.8
  467.9 3.2 fusion.4
  471.1 3.1 broadcast_select_fusion
  474.3 0.9 dynamic-slice_select_fusion.1
  475.4 423.7 %all-gather.11.cloned.1.call-done = f32[256,256,256]{2,1,0:T(8,128)} async-done(((f32[8,256,256]{2,1,0:T(8,128)}), f32[256,256,256]{2,1,0:T(8,128)}) %all-gather.11.cloned.1.call-update) | async-done | bytes 67108880 | tf_op jit(solution)/shard_map/all_gather | solution.py:12
  899.1 23.0 %reduce_sum.37 = f32[8,256,256]{2,1,0:T(8,128)} reduce(f32[32,8,256,256]{3,2,1,0:T(8,128)} %bitcast.16, f32[]{:T(128)} %constant.47.clone.1), dimensions={0}, to_apply=%region_5.6 | reduce | flops 16252928 | bytes 69206016 | tf_op jit(solution)/shard_map/reduce_sum | solution.py:12
  922.1 1.9 dynamic-slice_select_fusion
  924.1 2.8 gather_fusion
  926.9 7.2 all-gather.13.cloned.1.call-done
  934.0 2.5 reduce_sum.38
  936.6 2.8 gather_fusion.2
  939.3 4.3 gather_fusion.1
  943.7 26.8 %all-gather.15.cloned.1.call-done = f32[16,256,256]{2,1,0:T(8,128)} async-done(((f32[2,256,256]{2,1,0:T(8,128)}), f32[16,256,256]{2,1,0:T(8,128)}) %all-gather.15.cloned.1.call-update) | async-done | bytes 4194320 | tf_op jit(solution)/shard_map/all_gather | solution.py:12
  970.4 2.5 reduce_sum.39
  973.0 2.8 gather_fusion.3
  975.8 22.5 %bitcast_subtract_fusion = f32[16,256,256]{2,1,0:T(8,128)S(1)} fusion(f32[16,1,256,256]{3,2,1,0:T(8,128)} %param.9, pred[16]{0:T(512)(128)(4,1)S(1)} %compare_bitcast_fusion.1, f32[16,256,256]{2,1,0:T(8,128)} %gather_fusion.3, f32[16,256,256]{2,1,0:T(8,128)} %gather_fusion.2, f32[16,256,256]{2,1,0:T(8,128)} %gather_fusion.1, f32[16,256,256]{2,1,0:T(8,128)} %gather_fusion), kind=kOutput, calls=%fused_computation.23 | convolution fusion | flops 6448742400 | bytes 25165840 | tf_op jit(solution)/shard_map/sak,sbk->sab/dot_general | solution.py:60
  998.3 0.6 slice_select_fusion
  998.9 2.4 maximum_bitcast_fusion
  (32 shorter events, 1.0 us)
Async XLA Ops:
  6.5 5.4 copy-start
  6.5 438.5 %all-gather.9.cloned.1.call-start = ((), (), s32[]{:S(2)}) async-start(), calls=%async_computation | async-start | bytes 69206016 | tf_op jit(solution)/shard_map/all_gather | solution.py:12
  6.5 3.1 copy-start.6
  6.5 3.1 copy-start.5
  9.9 1.9 copy-start.1
  11.8 887.3 %all-gather.11.cloned.1.call-start = ((), (), s32[]{:S(2)}) async-start(), calls=%async_computation.1 | async-start | bytes 69206016 | tf_op jit(solution)/shard_map/all_gather | solution.py:12
  465.9 2.0 copy-start.4
  474.2 459.8 %all-gather.13.cloned.1.call-start = ((), (), s32[]{:S(2)}) async-start(), calls=%async_computation.2 | async-start | bytes 4718592 | tf_op jit(solution)/shard_map/all_gather | solution.py:12
  475.2 495.2 %all-gather.15.cloned.1.call-start = ((), (), s32[]{:S(2)}) async-start(), calls=%async_computation.3 | async-start | bytes 4718592 | tf_op jit(solution)/shard_map/all_gather | solution.py:12
  899.1 24.9 %copy-start.7 = (s32[2,16,1]{1,2,0:T(1,128)S(1)}, s32[2,16,1]{1,2,0:T(1,128)}, u32[]{:S(2)}) copy-start(s32[2,16,1]{1,2,0:T(1,128)} %param.11) | copy-start | bytes 388
  975.8 22.5 %copy-start.2 = (f32[8,256,256]{2,1,0:T(8,128)S(1)}, f32[8,256,256]{2,1,0:T(8,128)}, u32[]{:S(2)}) copy-start(f32[8,256,256]{2,1,0:T(8,128)} %copy-done.1) | copy-start | bytes 6291460
  975.8 22.5 %copy-start.3 = (f32[8,256,256]{2,1,0:T(8,128)S(1)}, f32[8,256,256]{2,1,0:T(8,128)}, u32[]{:S(2)}) copy-start(f32[8,256,256]{2,1,0:T(8,128)} %get-tuple-element.51) | copy-start | bytes 6291460
Sparse Core Ops, SparseCore 0:
  12.0 433.0 all-gather.8
  474.3 424.7 all-gather.10
  901.0 33.0 all-gather.12
  935.8 34.6 all-gather.14
